TPU v7x, 128 devices: a whole 4x4x4 slice. The times are simulated.
128 devices in a mesh: dom: 8 (over x, z_hi), grid: 16 (over z_lo, y, core).
Axes of the slice: x: 4, y: 4, z: 4 (z_hi: 2, z_lo: 2; z = z_hi * 2 + z_lo), core: 2. Of those that a mesh axis runs over, the one named last changes fastest.
Arguments:
- bands: float32 [8, 4, 64, 48, 1280], P('dom', None, None, 'grid'), may hold values from -6 to 6
- potential: float32 [4, 48, 32, 256], P(None, 'grid', 'dom'), may hold values from -1 to 1
- domain_blocks: int32 [8, 6], replicated, may hold values from 0 to 31, as said below
- block_slots: int32 [32], replicated, may hold values from 0 to 31, as said below
- domain_offsets: int32 [8], replicated, may hold values from 0 to 3
Outputs:
- filtered: float32 [8, 4, 64, 48, 1280], P('dom', None, None, 'grid')
Inputs may be any that keep to these rules, and one draw needn't show every extreme that they name: `domain_blocks`: each row is 6 cyclically consecutive logical blocks. `block_slots`: a permutation; slot // 4 is the index of dom that stores the block; no domain has more than 1 of its blocks stored on one index of dom, and some domain has exactly 1.
All inputs are finite; a program needn't handle non-finite values.
Results may differ from a plain program's by a relative error of at most 0.0003.
Values sent between devices are 32-bit elements; how exact they have to be, the bound alone decides.
No kernel may reach another device: no remote copies, remote signals or barrier semaphores. Data moves between devices by JAX's collectives and lax.ppermute only.
A program may use at most 128 MiB of HBM per device.

v0:
```python
import jax
import jax.numpy as jnp
from jax import lax
from jax.sharding import PartitionSpec as P

DZ = 64
OVL = 6
CELLS = 1280
e_half = 4.5
centre = 5.0
sigma_one = e_half / (-3.5 - centre)
sigma_two = 1.0 / (2.0 / sigma_one - sigma_one)
sigma_three = 1.0 / (2.0 / sigma_one - sigma_two)
rashba = 0.3


def extended(block, sides, width):
    for axis, dim in sides:
        count = lax.axis_size(axis)
        forward = [(i, i + 1) for i in range(count - 1)]
        backward = [(target, source) for source, target in forward]
        low = lax.ppermute(
            lax.slice_in_dim(block, block.shape[dim] - width, None, axis=dim), axis, forward
        )
        high = lax.ppermute(lax.slice_in_dim(block, 0, width, axis=dim), axis, backward)
        block = jnp.concatenate([low, block, high], axis=dim)
    return block


def along(field, steps):
    zeros = jnp.zeros(field.shape[:-1] + (abs(steps),), jnp.float32)
    if steps > 0:
        return jnp.concatenate([field[..., steps:], zeros], axis=-1)
    return jnp.concatenate([zeros, field[..., :steps]], axis=-1)


def apply_h(padded, fields):
    middle = padded[:, :, 1:-1]
    x_next = padded[:, :, 2:]
    x_prev = padded[:, :, :-2]
    cell_ids = jnp.arange(middle.shape[-1]) % DZ
    z_high = (cell_ids != DZ - 1).astype(jnp.float32)
    z_low = (cell_ids != 0).astype(jnp.float32)
    y_next = along(middle, DZ)
    y_prev = along(middle, -DZ)
    z_next = along(middle, 1) * z_high
    z_prev = along(middle, -1) * z_low
    lapl = x_next + x_prev + y_next + y_prev + z_next + z_prev - 6.0 * middle
    diff_x = 0.5 * (x_next - x_prev)
    diff_y = 0.5 * (y_next - y_prev)
    pot_v, mag_x, mag_y, mag_z = (
        fields[0][None],
        fields[1][None],
        fields[2][None],
        fields[3][None],
    )
    a_up, b_up, a_dn, b_dn = (middle[0], middle[1], middle[2], middle[3])
    out_a = (
        -0.5 * lapl[0]
        + pot_v * a_up
        + mag_z * a_up
        + mag_x * a_dn
        + mag_y * b_dn
        + rashba * (diff_y[3] + diff_x[2])
    )
    out_b = (
        -0.5 * lapl[1]
        + pot_v * b_up
        + mag_z * b_up
        + mag_x * b_dn
        - mag_y * a_dn
        + rashba * (diff_x[3] - diff_y[2])
    )
    out_c = (
        -0.5 * lapl[2]
        + pot_v * a_dn
        + mag_x * a_up
        - mag_y * b_up
        - mag_z * a_dn
        + rashba * (diff_y[1] - diff_x[0])
    )
    out_d = (
        -0.5 * lapl[3]
        + pot_v * b_dn
        + mag_x * b_up
        + mag_y * a_up
        - mag_z * b_dn
        - rashba * (diff_y[0] + diff_x[1])
    )
    return jnp.stack([out_a, out_b, out_c, out_d])


def neighbours(field):
    return extended(field, (("grid", 2),), 1)


def per_device(bands, potential, domain_blocks, block_slots, domain_offsets):
    spinors = bands[0]
    planes = spinors.shape[2]
    block_cells = potential.shape[3]
    domain = lax.axis_index("dom")
    slot_ids = block_slots[domain_blocks]
    gathered = lax.all_gather(potential, "dom", axis=2, tiled=True)
    picked = jnp.take(gathered, slot_ids[domain], axis=2)
    window = picked.reshape(4, planes, OVL * block_cells)
    first_cell = domain_offsets[domain] * DZ
    fields = lax.dynamic_slice_in_dim(window, first_cell, CELLS, 2)
    first = sigma_one / e_half * (apply_h(neighbours(spinors), fields) - centre * spinors)
    second = (
        2.0 * sigma_two / e_half * (apply_h(neighbours(first), fields) - centre * first)
        - sigma_one * sigma_two * spinors
    )
    third = (
        2.0 * sigma_three / e_half * (apply_h(neighbours(second), fields) - centre * second)
        - sigma_two * sigma_three * first
    )
    return third[None]


def solution(mesh):
    placed = (P("dom", None, None, "grid", None), P(None, "grid", "dom", None), P(), P(), P())
    return jax.shard_map(
        per_device,
        mesh=mesh,
        in_specs=placed,
        out_specs=P("dom", None, None, "grid", None),
        check_vma=False,
    )
```

profile of v0, /device:TPU:25, one launch (start us, length us, event | category | flops | bytes accessed | tf_op | source)
XLA Modules:
  0.0 171.0 jit_solution(2017998420111669350)
XLA Ops:
  0.0 0.0 copy-start
  0.0 2.0 %fusion.99 = (f32[4,64,1,1280]{3,1,2,0:T(8,128)S(1)}, f32[4,64,1,1280]{3,1,2,0:T(8,128)S(1)}) fusion(f32[4,64,3,1280]{3,1,2,0:T(8,128)} %bitcast.95), kind=kLoop, calls=%fused_computation.176 | loop fusion | bytes 5242880 | tf_op jit(solution)/shard_map/slice | solution.py:23
  2.0 3.8 %collective-permute-start.1 = (f32[4,64,1,1280]{3,1,2,0:T(8,128)S(1)}, f32[4,64,1,1280]{3,1,2,0:T(8,128)}, u32[]{:S(2)}, u32[]{:S(2)}) collective-permute-start(f32[4,64,1,1280]{3,1,2,0:T(8,128)S(1)} %get-tuple-element.41), channel_id=1, source_target_pairs={{0,1},{1,2},{2,3},{3,4},{4,5},{5,6},{6,7},{7,8},{8,9},{9,10},{10,1... | collective-permute-start | bytes 3932168 | tf_op jit(solution)/shard_map/ppermute | solution.py:22
  5.8 1.9 %collective-permute-start = (f32[4,64,1,1280]{3,1,2,0:T(8,128)S(1)}, f32[4,64,1,1280]{3,1,2,0:T(8,128)}, u32[]{:S(2)}, u32[]{:S(2)}) collective-permute-start(f32[4,64,1,1280]{3,1,2,0:T(8,128)S(1)} %get-tuple-element.42), channel_id=1, source_target_pairs={{1,0},{2,1},{3,2},{4,3},{5,4},{6,5},{7,6},{8,7},{9,8},{10,9},{11,1... | collective-permute-start | bytes 3932168 | tf_op jit(solution)/shard_map/ppermute | solution.py:25
  7.7 0.0 copy-done.19
  7.7 0.1 reshape.232
  7.8 0.0 copy-done
  7.8 0.8 gather_fusion
  8.6 0.1 reshape.231
  8.7 0.0 copy-start.20
  8.7 0.0 copy-start.18
  8.8 7.6 %fusion.97 = (f32[4,64,3,1279]{3,1,2,0:T(8,128)}, f32[4,64,3,1279]{3,1,2,0:T(8,128)}) fusion(f32[4,64,3,1280]{3,1,2,0:T(8,128)} %bitcast.96), kind=kLoop, calls=%fused_computation.174 | loop fusion | bytes 15716352 | tf_op jit(solution)/shard_map/slice | solution.py:33
  16.4 0.0 copy-done.20
  16.4 0.6 dynamic_slice.10
  17.7 0.1 broadcast_in_dim.25
  17.8 28.8 %all_gather.3 = f32[4,3,32,256]{3,0,2,1:T(4,128)S(1)} all-gather(f32[4,3,4,256]{3,0,2,1:T(4,128)S(1)} %copy.6), channel_id=1, replica_groups=mesh['dom'=8,'grid'=16] {'dom'}, dimensions={2}, use_global_device_ids=true | all-gather | bytes 442368 | tf_op jit(solution)/shard_map/all_gather | solution.py:103
  46.6 0.6 gather_fusion.1
  47.2 0.1 dynamic-slice
  47.3 0.1 dynamic-slice_select_fusion
  47.5 0.0 copy-start.2
  47.5 0.0 copy-start.11
  47.5 7.7 %fusion.98 = (f32[4,64,3,1216]{3,1,2,0:T(8,128)}, f32[4,64,3,1216]{3,1,2,0:T(8,128)}) fusion(f32[4,64,3,1280]{3,1,2,0:T(8,128)} %bitcast.97), kind=kLoop, calls=%fused_computation.175 | loop fusion | bytes 14942208 | tf_op jit(solution)/shard_map/slice | solution.py:33
  55.3 0.0 collective-permute-done.1
  55.3 0.0 collective-permute-done
  55.3 8.5 %multiply_subtract_fusion.2 = (f32[4,64,3,1280]{3,1,2,0:T(8,128)S(1)}, f32[4,64,3,1280]{3,1,2,0:T(8,128)}, f32[4,64,3,1280]{3,1,2,0:T(8,128)}) fusion(f32[4,64,3,1280]{3,1,2,0:T(8,128)S(1)} %bitcast.98, f32[4,64,3,1279]{3,1,2,0:T(8,128)} %get-tuple-element.38, f32[4,64,3,1279]{3,1,2,0:T(8,128)S(1)} %copy-done.11, f32[4,64,3,1216]{3,1,2,0:T(8,128)} %get-tuple-element.40, ...), kind=kLoop, calls=%fused_computation.28 | loop fusion | flops 14745600 | bytes 33689600 | tf_op jit(solution)/shard_map/sub | solution.py:48
  63.8 3.5 %fusion.72 = (f32[1,64,3,1280]{3,1,2,0:T(8,128)S(1)}, f32[1,64,3,1280]{3,1,2,0:T(8,128)S(1)}) fusion(f32[4,64,3,1280]{3,1,2,0:T(8,128)} %get-tuple-element.22, f32[4,64,3,1280]{3,1,2,0:T(8,128)} %get-tuple-element.24, f32[4,64,3,1280]{3,1,2,0:T(8,128)S(1)} %get-tuple-element.21, f32[1,4,64,3,1280]{4,2,3,1,0:T(8,128)S(1)} %copy-done.2, ...), kind=kLoop, calls=%fused_computation.116 | loop fusion | flops 5898240 | bytes 11857920 | tf_op jit(solution)/shard_map/add | solution.py:67
  67.3 0.0 copy-done.9
  67.3 1.0 copy-done.10
  68.3 1.1 fusion.78
  69.4 0.6 broadcast_multiply_fusion
  69.9 0.2 fusion.96
  70.1 11.8 %collective-permute-start.3 = (f32[4,64,1,1280]{3,1,2,0:T(8,128)S(1)}, f32[4,64,1,1280]{3,1,2,0:T(8,128)S(1)}, u32[]{:S(2)}, u32[]{:S(2)}) collective-permute-start(f32[4,64,1,1280]{3,1,2,0:T(8,128)S(1)} %get-tuple-element.35), channel_id=1, source_target_pairs={{0,1},{1,2},{2,3},{3,4},{4,5},{5,6},{6,7},{7,8},{8,9},{9,10},{10,1... | collective-permute-start | bytes 3932168 | tf_op jit(solution)/shard_map/ppermute | solution.py:22
  82.0 2.1 %collective-permute-start.2 = (f32[4,64,1,1280]{3,1,2,0:T(8,128)S(1)}, f32[4,64,1,1280]{3,1,2,0:T(8,128)S(1)}, u32[]{:S(2)}, u32[]{:S(2)}) collective-permute-start(f32[4,64,1,1280]{3,1,2,0:T(8,128)S(1)} %get-tuple-element.36), channel_id=1, source_target_pairs={{1,0},{2,1},{3,2},{4,3},{5,4},{6,5},{7,6},{8,7},{9,8},{10,9},{11,1... | collective-permute-start | bytes 3932168 | tf_op jit(solution)/shard_map/ppermute | solution.py:25
  84.1 4.4 %fusion.94 = (f32[4,64,3,1279]{3,1,2,0:T(8,128)}, f32[4,64,3,1279]{3,1,2,0:T(8,128)}) fusion(f32[4,64,3,1280]{3,1,2,0:T(8,128)S(1)} %broadcast_multiply_fusion), kind=kLoop, calls=%fused_computation.171 | loop fusion | bytes 15716352 | tf_op jit(solution)/shard_map/slice | solution.py:33
  88.5 4.4 %fusion.95 = (f32[4,64,3,1216]{3,1,2,0:T(8,128)}, f32[4,64,3,1216]{3,1,2,0:T(8,128)}) fusion(f32[4,64,3,1280]{3,1,2,0:T(8,128)S(1)} %broadcast_multiply_fusion), kind=kLoop, calls=%fused_computation.172 | loop fusion | bytes 14942208 | tf_op jit(solution)/shard_map/slice | solution.py:33
  93.0 3.6 %collective-permute-done.3 = f32[4,64,1,1280]{3,1,2,0:T(8,128)S(1)} collective-permute-done((f32[4,64,1,1280]{3,1,2,0:T(8,128)S(1)}, f32[4,64,1,1280]{3,1,2,0:T(8,128)S(1)}, u32[]{:S(2)}, u32[]{:S(2)}) %collective-permute-start.3) | collective-permute-done | bytes 1310752 | tf_op jit(solution)/shard_map/ppermute | solution.py:22
  96.5 6.5 %collective-permute-done.2 = f32[4,64,1,1280]{3,1,2,0:T(8,128)S(1)} collective-permute-done((f32[4,64,1,1280]{3,1,2,0:T(8,128)S(1)}, f32[4,64,1,1280]{3,1,2,0:T(8,128)S(1)}, u32[]{:S(2)}, u32[]{:S(2)}) %collective-permute-start.2) | collective-permute-done | bytes 1310752 | tf_op jit(solution)/shard_map/ppermute | solution.py:25
  103.0 2.5 %subtract_multiply_fusion.2 = f32[4,64,3,1280]{3,1,2,0:T(8,128)} fusion(f32[4,64,1,1280]{3,1,2,0:T(8,128)S(1)} %collective-permute-done.2, f32[4,64,3,1280]{3,1,2,0:T(8,128)S(1)} %broadcast_multiply_fusion, f32[4,64,1,1280]{3,1,2,0:T(8,128)S(1)} %collective-permute-done.3), kind=kLoop, calls=%fused_computation.23 | loop fusion | flops 3932160 | bytes 10485760 | tf_op jit(solution)/shard_map/mul | solution.py:49
  105.5 9.3 %multiply_subtract_fusion.1 = (f32[4,64,3,1280]{3,1,2,0:T(8,128)}, f32[4,64,3,1280]{3,1,2,0:T(8,128)}) fusion(f32[4,64,3,1279]{3,1,2,0:T(8,128)} %get-tuple-element.32, f32[4,64,3,1279]{3,1,2,0:T(8,128)} %get-tuple-element.31, f32[4,64,3,1216]{3,1,2,0:T(8,128)} %get-tuple-element.34, f32[4,64,3,1216]{3,1,2,0:T(8,128)} %get-tuple-element.33, ...), kind=kLoop, calls=%fused_computation.25 | loop fusion | flops 17694720 | bytes 37621760 | tf_op jit(solution)/shard_map/sub | solution.py:48
  114.8 4.1 %fusion.48 = (f32[1,64,3,1280]{3,1,2,0:T(8,128)S(1)}, f32[1,64,3,1280]{3,1,2,0:T(8,128)S(1)}) fusion(f32[4,64,3,1280]{3,1,2,0:T(8,128)} %get-tuple-element.20, f32[4,64,3,1280]{3,1,2,0:T(8,128)} %subtract_multiply_fusion.2, f32[4,64,3,1280]{3,1,2,0:T(8,128)} %get-tuple-element.19, f32[4,64,3,1280]{3,1,2,0:T(8,128)S(1)} %broadcast_multiply_fusion, ...), kind=kLoop, calls=%fused_computation.84 | loop fusion | flops 5898240 | bytes 11857920 | tf_op jit(solution)/shard_map/add | solution.py:67
  118.9 0.0 copy-done.3
  118.9 1.0 copy-done.4
  119.9 1.1 copy-done.5
  121.0 1.0 fusion.54
  122.0 1.1 fusion.1
  123.1 0.0 copy-done.12
  123.2 0.1 copy-done.14
  123.2 0.2 fusion.93
  123.5 1.9 %collective-permute-start.5 = (f32[4,64,1,1280]{3,1,2,0:T(8,128)S(1)}, f32[4,64,1,1280]{3,1,2,0:T(8,128)S(1)}, u32[]{:S(2)}, u32[]{:S(2)}) collective-permute-start(f32[4,64,1,1280]{3,1,2,0:T(8,128)S(1)} %get-tuple-element.29), channel_id=1, source_target_pairs={{0,1},{1,2},{2,3},{3,4},{4,5},{5,6},{6,7},{7,8},{8,9},{9,10},{10,1... | collective-permute-start | bytes 3932168 | tf_op jit(solution)/shard_map/ppermute | solution.py:22
  125.4 2.6 %collective-permute-start.4 = (f32[4,64,1,1280]{3,1,2,0:T(8,128)S(1)}, f32[4,64,1,1280]{3,1,2,0:T(8,128)S(1)}, u32[]{:S(2)}, u32[]{:S(2)}) collective-permute-start(f32[4,64,1,1280]{3,1,2,0:T(8,128)S(1)} %get-tuple-element.30), channel_id=1, source_target_pairs={{1,0},{2,1},{3,2},{4,3},{5,4},{6,5},{7,6},{8,7},{9,8},{10,9},{11,1... | collective-permute-start | bytes 3932168 | tf_op jit(solution)/shard_map/ppermute | solution.py:25
  128.0 4.5 %fusion.92 = (f32[4,64,3,1216]{3,1,2,0:T(8,128)}, f32[4,64,3,1216]{3,1,2,0:T(8,128)}) fusion(f32[4,64,3,1280]{3,1,2,0:T(8,128)S(1)} %fusion.1), kind=kLoop, calls=%fused_computation.169 | loop fusion | bytes 14942208 | tf_op jit(solution)/shard_map/slice | solution.py:33
  132.5 4.5 %fusion.91 = (f32[4,64,3,1279]{3,1,2,0:T(8,128)}, f32[4,64,3,1279]{3,1,2,0:T(8,128)}) fusion(f32[4,64,3,1280]{3,1,2,0:T(8,128)S(1)} %fusion.1), kind=kLoop, calls=%fused_computation.168 | loop fusion | bytes 15716352 | tf_op jit(solution)/shard_map/slice | solution.py:33
  137.1 2.9 %collective-permute-done.5 = f32[4,64,1,1280]{3,1,2,0:T(8,128)S(1)} collective-permute-done((f32[4,64,1,1280]{3,1,2,0:T(8,128)S(1)}, f32[4,64,1,1280]{3,1,2,0:T(8,128)S(1)}, u32[]{:S(2)}, u32[]{:S(2)}) %collective-permute-start.5) | collective-permute-done | bytes 1310752 | tf_op jit(solution)/shard_map/ppermute | solution.py:22
  139.9 6.5 %collective-permute-done.4 = f32[4,64,1,1280]{3,1,2,0:T(8,128)S(1)} collective-permute-done((f32[4,64,1,1280]{3,1,2,0:T(8,128)S(1)}, f32[4,64,1,1280]{3,1,2,0:T(8,128)S(1)}, u32[]{:S(2)}, u32[]{:S(2)}) %collective-permute-start.4) | collective-permute-done | bytes 1310752 | tf_op jit(solution)/shard_map/ppermute | solution.py:25
  146.4 1.2 copy-done.17
  147.6 10.7 %multiply_subtract_fusion = (f32[4,64,3,1280]{3,1,2,0:T(8,128)}, f32[4,64,3,1280]{3,1,2,0:T(8,128)}, f32[4,64,3,1280]{3,1,2,0:T(8,128)}) fusion(f32[4,64,3,1280]{3,1,2,0:T(8,128)S(1)} %fusion.1, f32[4,64,3,1279]{3,1,2,0:T(8,128)} %get-tuple-element.26, f32[4,64,3,1279]{3,1,2,0:T(8,128)} %get-tuple-element.25, f32[4,64,3,1216]{3,1,2,0:T(8,128)} %get-tuple-element.28, ...), kind=kLoop, calls=%fused_computation.22 | loop fusion | flops 14745600 | bytes 33689600 | tf_op jit(solution)/shard_map/sub | solution.py:48
  158.3 0.0 copy-start.7
  158.3 0.0 copy-start.8
  158.4 4.1 %fusion.23 = (f32[1,1,64,3,1280]{4,2,3,1,0:T(8,128)S(1)}, f32[1,1,64,3,1280]{4,2,3,1,0:T(8,128)S(1)}) fusion(f32[4,64,3,1280]{3,1,2,0:T(8,128)} %get-tuple-element.18, f32[4,64,3,1280]{3,1,2,0:T(8,128)} %get-tuple-element.23, f32[4,64,3,1280]{3,1,2,0:T(8,128)} %get-tuple-element.17, f32[4,64,3,1280]{3,1,2,0:T(8,128)S(1)} %fusion.1, ...), kind=kLoop, calls=%fused_computation.51 | loop fusion | flops 5898240 | bytes 11857920 | tf_op jit(solution)/shard_map/stack | solution.py:90
  162.4 1.0 copy-done.7
  163.4 1.1 copy-done.8
  164.5 2.0 %fusion.30 = (f32[1,1,64,3,1280]{4,2,3,1,0:T(8,128)S(1)}, f32[1,1,64,3,1280]{4,2,3,1,0:T(8,128)}) fusion(f32[4,64,3,1280]{3,1,2,0:T(8,128)S(1)} %copy-done.8, f32[4,64,3,1280]{3,1,2,0:T(8,128)S(1)} %copy-done.7, f32[4,64,3,1280]{3,1,2,0:T(8,128)S(1)} %copy-done.6, f32[4,64,3,1280]{3,1,2,0:T(8,128)S(1)} %fusion.1, f32[3,1280]{1,0:T(4,128)S(1)} %get-tuple-element.49, ...), kind=kLoop, calls=%fused_computation.60 | loop fusion | flops 5898240 | bytes 11857920 | tf_op jit(solution)/shard_map/stack | solution.py:90
  166.5 4.5 %fusion.3 = f32[1,4,64,3,1280]{4,2,3,1,0:T(8,128)} fusion(f32[1,1,64,3,1280]{4,2,3,1,0:T(8,128)} %get-tuple-element.6, f32[1,1,64,3,1280]{4,2,3,1,0:T(8,128)S(1)} %get-tuple-element.8, f32[1,1,64,3,1280]{4,2,3,1,0:T(8,128)S(1)} %get-tuple-element.7, f32[1,1,64,3,1280]{4,2,3,1,0:T(8,128)S(1)} %get-tuple-element.5, f32[1,1,64,3,1280]{4,2,3,1,0:T(8,128)S(1)} %bitcast.106, ...), kind=kLoop, calls=%fused_computation.14 | loop fusion | flops 20643840 | bytes 19660800 | tf_op jit(solution)/shard_map/sub | solution.py:114
  171.0 0.0 copy-done.1
  (33 shorter events, 0.2 us)
Async XLA Ops:
  0.0 7.8 %copy-start = (s32[32]{0:T(128)S(1)}, s32[32]{0:T(128)}, u32[]{:S(2)}) copy-start(s32[32]{0:T(128)} %param.8) | copy-start | bytes 388
  0.0 7.7 %copy-start.19 = (s32[8,6]{1,0:T(8,128)S(1)}, s32[8,6]{1,0:T(8,128)}, u32[]{:S(2)}) copy-start(s32[8,6]{1,0:T(8,128)} %param.7) | copy-start | bytes 580
  2.0 53.3 %collective-permute-start.1 = (f32[4,64,1,1280]{3,1,2,0:T(8,128)S(1)}, f32[4,64,1,1280]{3,1,2,0:T(8,128)}, u32[]{:S(2)}, u32[]{:S(2)}) collective-permute-start(f32[4,64,1,1280]{3,1,2,0:T(8,128)S(1)} %get-tuple-element.41), channel_id=1, source_target_pairs={{0,1},{1,2},{2,3},{3,4},{4,5},{5,6},{6,7},{7,8},{8,9},{9,10},{10,1... | collective-permute-start | bytes 3932168 | tf_op jit(solution)/shard_map/ppermute | solution.py:22
  5.8 49.5 %collective-permute-start = (f32[4,64,1,1280]{3,1,2,0:T(8,128)S(1)}, f32[4,64,1,1280]{3,1,2,0:T(8,128)}, u32[]{:S(2)}, u32[]{:S(2)}) collective-permute-start(f32[4,64,1,1280]{3,1,2,0:T(8,128)S(1)} %get-tuple-element.42), channel_id=1, source_target_pairs={{1,0},{2,1},{3,2},{4,3},{5,4},{6,5},{7,6},{8,7},{9,8},{10,9},{11,1... | collective-permute-start | bytes 3932168 | tf_op jit(solution)/shard_map/ppermute | solution.py:25
  8.7 7.7 %copy-start.20 = (s32[8]{0:T(128)S(1)}, s32[8]{0:T(128)}, u32[]{:S(2)}) copy-start(s32[8]{0:T(128)} %param.9) | copy-start | bytes 100
  8.7 9.0 %copy-start.18 = (f32[4,3,4,256]{3,2,1,0:T(4,128)S(1)}, f32[4,3,4,256]{3,2,1,0:T(4,128)}, u32[]{:S(2)}) copy-start(f32[4,3,4,256]{3,2,1,0:T(4,128)} %param.6) | copy-start | bytes 147460
  47.5 7.8 %copy-start.2 = (f32[1,4,64,3,1280]{4,2,3,1,0:T(8,128)S(1)}, f32[1,4,64,3,1280]{4,2,3,1,0:T(8,128)}, u32[]{:S(2)}) copy-start(f32[1,4,64,3,1280]{4,2,3,1,0:T(8,128)} %param.5) | copy-start | bytes 11796484
  47.5 7.8 %copy-start.11 = (f32[4,64,3,1279]{3,1,2,0:T(8,128)S(1)}, f32[4,64,3,1279]{3,1,2,0:T(8,128)}, u32[]{:S(2)}) copy-start(f32[4,64,3,1279]{3,1,2,0:T(8,128)} %get-tuple-element.37) | copy-start | bytes 11787268
  63.8 3.5 %copy-start.9 = (f32[4,64,3,1280]{3,1,2,0:T(8,128)S(1)}, f32[4,64,3,1280]{3,1,2,0:T(8,128)}, u32[]{:S(2)}) copy-start(f32[4,64,3,1280]{3,1,2,0:T(8,128)} %get-tuple-element.22) | copy-start | bytes 11796484
  63.8 4.5 %copy-start.10 = (f32[4,64,3,1280]{3,1,2,0:T(8,128)S(1)}, f32[4,64,3,1280]{3,1,2,0:T(8,128)}, u32[]{:S(2)}) copy-start(f32[4,64,3,1280]{3,1,2,0:T(8,128)} %get-tuple-element.24) | copy-start | bytes 11796484
  70.1 26.4 %collective-permute-start.3 = (f32[4,64,1,1280]{3,1,2,0:T(8,128)S(1)}, f32[4,64,1,1280]{3,1,2,0:T(8,128)S(1)}, u32[]{:S(2)}, u32[]{:S(2)}) collective-permute-start(f32[4,64,1,1280]{3,1,2,0:T(8,128)S(1)} %get-tuple-element.35), channel_id=1, source_target_pairs={{0,1},{1,2},{2,3},{3,4},{4,5},{5,6},{6,7},{7,8},{8,9},{9,10},{10,1... | collective-permute-start | bytes 3932168 | tf_op jit(solution)/shard_map/ppermute | solution.py:22
  82.0 21.0 %collective-permute-start.2 = (f32[4,64,1,1280]{3,1,2,0:T(8,128)S(1)}, f32[4,64,1,1280]{3,1,2,0:T(8,128)S(1)}, u32[]{:S(2)}, u32[]{:S(2)}) collective-permute-start(f32[4,64,1,1280]{3,1,2,0:T(8,128)S(1)} %get-tuple-element.36), channel_id=1, source_target_pairs={{1,0},{2,1},{3,2},{4,3},{5,4},{6,5},{7,6},{8,7},{9,8},{10,9},{11,1... | collective-permute-start | bytes 3932168 | tf_op jit(solution)/shard_map/ppermute | solution.py:25
  114.8 4.1 %copy-start.3 = (f32[4,64,3,1280]{3,1,2,0:T(8,128)S(1)}, f32[4,64,3,1280]{3,1,2,0:T(8,128)}, u32[]{:S(2)}) copy-start(f32[4,64,3,1280]{3,1,2,0:T(8,128)} %subtract_multiply_fusion.2) | copy-start | bytes 11796484
  114.8 5.1 %copy-start.4 = (f32[4,64,3,1280]{3,1,2,0:T(8,128)S(1)}, f32[4,64,3,1280]{3,1,2,0:T(8,128)}, u32[]{:S(2)}) copy-start(f32[4,64,3,1280]{3,1,2,0:T(8,128)} %get-tuple-element.19) | copy-start | bytes 11796484
  114.8 6.2 %copy-start.5 = (f32[4,64,3,1280]{3,1,2,0:T(8,128)S(1)}, f32[4,64,3,1280]{3,1,2,0:T(8,128)}, u32[]{:S(2)}) copy-start(f32[4,64,3,1280]{3,1,2,0:T(8,128)} %get-tuple-element.20) | copy-start | bytes 11796484
  122.0 1.2 copy-start.12
  122.0 1.2 copy-start.14
  123.5 16.5 %collective-permute-start.5 = (f32[4,64,1,1280]{3,1,2,0:T(8,128)S(1)}, f32[4,64,1,1280]{3,1,2,0:T(8,128)S(1)}, u32[]{:S(2)}, u32[]{:S(2)}) collective-permute-start(f32[4,64,1,1280]{3,1,2,0:T(8,128)S(1)} %get-tuple-element.29), channel_id=1, source_target_pairs={{0,1},{1,2},{2,3},{3,4},{4,5},{5,6},{6,7},{7,8},{8,9},{9,10},{10,1... | collective-permute-start | bytes 3932168 | tf_op jit(solution)/shard_map/ppermute | solution.py:22
  125.4 21.0 %collective-permute-start.4 = (f32[4,64,1,1280]{3,1,2,0:T(8,128)S(1)}, f32[4,64,1,1280]{3,1,2,0:T(8,128)S(1)}, u32[]{:S(2)}, u32[]{:S(2)}) collective-permute-start(f32[4,64,1,1280]{3,1,2,0:T(8,128)S(1)} %get-tuple-element.30), channel_id=1, source_target_pairs={{1,0},{2,1},{3,2},{4,3},{5,4},{6,5},{7,6},{8,7},{9,8},{10,9},{11,1... | collective-permute-start | bytes 3932168 | tf_op jit(solution)/shard_map/ppermute | solution.py:25
  139.9 6.5 %copy-start.16 = (f32[4,64,1,1280]{3,1,2,0:T(8,128)}, f32[4,64,1,1280]{3,1,2,0:T(8,128)S(1)}, u32[]{:S(2)}) copy-start(f32[4,64,1,1280]{3,1,2,0:T(8,128)S(1)} %collective-permute-done.5) | copy-start | bytes 3932164
  146.4 1.2 copy-start.17
  158.3 4.1 %copy-start.6 = (f32[4,64,3,1280]{3,1,2,0:T(8,128)S(1)}, f32[4,64,3,1280]{3,1,2,0:T(8,128)}, u32[]{:S(2)}) copy-start(f32[4,64,3,1280]{3,1,2,0:T(8,128)} %get-tuple-element.17) | copy-start | bytes 11796484
  158.3 5.1 %copy-start.7 = (f32[4,64,3,1280]{3,1,2,0:T(8,128)S(1)}, f32[4,64,3,1280]{3,1,2,0:T(8,128)}, u32[]{:S(2)}) copy-start(f32[4,64,3,1280]{3,1,2,0:T(8,128)} %get-tuple-element.18) | copy-start | bytes 11796484
  158.3 6.2 %copy-start.8 = (f32[4,64,3,1280]{3,1,2,0:T(8,128)S(1)}, f32[4,64,3,1280]{3,1,2,0:T(8,128)}, u32[]{:S(2)}) copy-start(f32[4,64,3,1280]{3,1,2,0:T(8,128)} %get-tuple-element.23) | copy-start | bytes 11796484
  164.5 2.0 %copy-start.13 = (f32[1,64,3,1280]{3,1,2,0:T(8,128)S(1)}, f32[1,64,3,1280]{3,1,2,0:T(8,128)}, u32[]{:S(2)}) copy-start(f32[1,64,3,1280]{3,1,2,0:T(8,128)} %copy-done.12) | copy-start | bytes 2949124
  164.5 2.0 %copy-start.15 = (f32[1,64,3,1280]{3,1,2,0:T(8,128)S(1)}, f32[1,64,3,1280]{3,1,2,0:T(8,128)}, u32[]{:S(2)}) copy-start(f32[1,64,3,1280]{3,1,2,0:T(8,128)} %copy-done.14) | copy-start | bytes 2949124
  166.5 4.5 %copy-start.1 = (s32[32]{0:T(128)S(1)}, s32[32]{0:T(128)}, u32[]{:S(2)}) copy-start(s32[32]{0:T(128)} %param.8) | copy-start | bytes 388
where the time goes:
time: 171 us
  other arithmetic  53 us (31%)
  local copies, waits for them, and re-layouts  44.6 us (26%)
  blocking collectives  28.8 us (17%)
  starting transfers between devices  24.2 us (14%)
  waiting for transfers between devices  19.4 us (11%)
    slice x6, local copies, waits for them, and re-layouts, along(): return jnp.concatenate([field[..., steps:], zeros], axis=-1)  33.3 us
    all_gather x1, blocking collectives, per_device(): gathered = lax.all_gather(potential, 'dom', axis=2, tiled=True)  28.8 us
    sub x3, other arithmetic, apply_h(): lapl = x_next + x_prev + y_next + y_prev + z_next + z_prev - 6.0 * middle  28.5 us
    ppermute x3, starting transfers between devices, extended(): lax.ppermute(lax.slice_in_dim(block, block.shape[dim] - width, None, axis...  17.5 us
    ppermute x3, waiting for transfers between devices, extended(): lax.ppermute(lax.slice_in_dim(block, 0, width, axis=dim), axis, backward)  13 us
    add x2, other arithmetic, apply_h(): -0.5 * lapl[1] + pot_v * b_up + mag_z * b_up + mag_x * b_dn - mag_y * a_dn  7.52 us
    ppermute x3, starting transfers between devices, extended(): lax.ppermute(lax.slice_in_dim(block, 0, width, axis=dim), axis, backward)  6.65 us
    unnamed x45, local copies, waits for them, and re-layouts  6.56 us
  transfers between devices with their start and end apart: 6, of which 4 were waited for; matrix products, arithmetic and copies ran while one was open for 21% of the time, Pallas kernels for 0%

commit v1 on v0

--- a/solution.py
+++ b/solution.py
@@ -100,7 +100,9 @@
     block_cells = potential.shape[3]
     domain = lax.axis_index("dom")
     slot_ids = block_slots[domain_blocks]
-    gathered = lax.all_gather(potential, "dom", axis=2, tiled=True)
+    gathered = jnp.concatenate(
+        lax.all_to_all(jnp.stack([potential] * lax.axis_size("dom")), "dom", 0, 0), axis=2
+    )
     picked = jnp.take(gathered, slot_ids[domain], axis=2)
     window = picked.reshape(4, planes, OVL * block_cells)
     first_cell = domain_offsets[domain] * DZ

time: 171 us -> 147 us (0.86)
  blocking collectives: 28.8 us -> 0 us
  waiting for transfers between devices: 19.4 us -> 25.9 us
  other arithmetic: 53 us -> 58 us
  local copies, waits for them, and re-layouts: 44.6 us -> 40 us
  starting transfers between devices: 24.2 us -> 21.5 us
    all_gather x1 -> x0, blocking collectives: 28.8 us -> none  [per_device(): gathered = lax.all_gather(potential, 'dom', axis=2, tiled=True)]
    ppermute x3, starting transfers between devices: 17.5 us -> 6.99 us  [extended(): lax.ppermute(lax.slice_in_dim(block, block.shape[dim] - width, None, axis...]
    all_to_all x0 -> x1, starting transfers between devices: none -> 7.33 us  [per_device(): lax.all_to_all(jnp.stack([potential] * lax.axis_size('dom')), 'dom', 0, 0)]
    ppermute x3, waiting for transfers between devices: 13 us -> 19.6 us  [extended(): lax.ppermute(lax.slice_in_dim(block, 0, width, axis=dim), axis, backward)]
    slice x6, local copies, waits for them, and re-layouts: 33.3 us -> 26.9 us  [along(): return jnp.concatenate([field[..., steps:], zeros], axis=-1)]
    sub x3, other arithmetic: 28.5 us -> 33.5 us  [apply_h(): lapl = x_next + x_prev + y_next + y_prev + z_next + z_prev - 6.0 * middle]
    unnamed x45 -> x43, local copies, waits for them, and re-layouts: 6.56 us -> 7.36 us
  transfers between devices with their start and end apart: 6 -> 7, of which waited for: 4 -> 6; matrix products, arithmetic and copies ran while one was open for 21% -> 22% of each run, Pallas kernels for 0% -> 0%
where the time goes in v1:
time: 147 us; the launch traced here: 146 us
  other arithmetic  58 us (39%)
  local copies, waits for them, and re-layouts  40 us (27%)
  waiting for transfers between devices  25.9 us (18%)
  starting transfers between devices  21.5 us (15%)
    sub x3, other arithmetic, apply_h(): lapl = x_next + x_prev + y_next + y_prev + z_next + z_prev - 6.0 * middle  33.5 us
    slice x6, local copies, waits for them, and re-layouts, along(): return jnp.concatenate([field[..., steps:], zeros], axis=-1)  26.9 us
    ppermute x3, waiting for transfers between devices, extended(): lax.ppermute(lax.slice_in_dim(block, 0, width, axis=dim), axis, backward)  19.6 us
    add x2, other arithmetic, apply_h(): -0.5 * lapl[1] + pot_v * b_up + mag_z * b_up + mag_x * b_dn - mag_y * a_dn  7.52 us
    unnamed x43, local copies, waits for them, and re-layouts  7.36 us
    all_to_all x1, starting transfers between devices, per_device(): lax.all_to_all(jnp.stack([potential] * lax.axis_size('dom')), 'dom', 0, 0)  7.33 us
    ppermute x3, starting transfers between devices, extended(): lax.ppermute(lax.slice_in_dim(block, 0, width, axis=dim), axis, backward)  7.14 us
    ppermute x3, starting transfers between devices, extended(): lax.ppermute(lax.slice_in_dim(block, block.shape[dim] - width, None, axis...  6.99 us
  transfers between devices with their start and end apart: 7, of which 6 were waited for; matrix products, arithmetic and copies ran while one was open for 22% of the time, Pallas kernels for 0%

profile of v1, /device:TPU:25, one launch (start us, length us, event | category | flops | bytes accessed | tf_op | source)
XLA Modules:
  0.0 146.3 jit_solution(8319654521154861921)
XLA Ops:
  0.0 0.0 copy-start
  0.0 0.8 copy.8
  0.8 0.8 stack.60
  1.7 7.3 %all-to-all-start = ((f32[8,4,3,4,256]{4,1,3,2,0:T(4,128)}), f32[8,4,3,4,256]{4,1,3,2,0:T(4,128)S(1)}, u32[]{:S(2)}, u32[]{:S(2)}) async-start(f32[8,4,3,4,256]{4,1,3,2,0:T(4,128)} %stack.60), calls=%async_computation | async-start | bytes 786432 | tf_op jit(solution)/shard_map/all_to_all | solution.py:104
  9.0 2.1 %fusion.99 = (f32[4,64,1,1280]{3,1,2,0:T(8,128)S(1)}, f32[4,64,1,1280]{3,1,2,0:T(8,128)S(1)}) fusion(f32[4,64,3,1280]{3,1,2,0:T(8,128)} %bitcast.97), kind=kLoop, calls=%fused_computation.176 | loop fusion | bytes 5242880 | tf_op jit(solution)/shard_map/slice | solution.py:23
  11.1 3.1 %collective-permute-start.1 = (f32[4,64,1,1280]{3,1,2,0:T(8,128)S(1)}, f32[4,64,1,1280]{3,1,2,0:T(8,128)}, u32[]{:S(2)}, u32[]{:S(2)}) collective-permute-start(f32[4,64,1,1280]{3,1,2,0:T(8,128)S(1)} %get-tuple-element.41), channel_id=1, source_target_pairs={{0,1},{1,2},{2,3},{3,4},{4,5},{5,6},{6,7},{7,8},{8,9},{9,10},{10,1... | collective-permute-start | bytes 3932168 | tf_op jit(solution)/shard_map/ppermute | solution.py:22
  14.3 1.9 %collective-permute-start = (f32[4,64,1,1280]{3,1,2,0:T(8,128)S(1)}, f32[4,64,1,1280]{3,1,2,0:T(8,128)}, u32[]{:S(2)}, u32[]{:S(2)}) collective-permute-start(f32[4,64,1,1280]{3,1,2,0:T(8,128)S(1)} %get-tuple-element.42), channel_id=1, source_target_pairs={{1,0},{2,1},{3,2},{4,3},{5,4},{6,5},{7,6},{8,7},{9,8},{10,9},{11,1... | collective-permute-start | bytes 3932168 | tf_op jit(solution)/shard_map/ppermute | solution.py:25
  16.2 0.0 copy-done.2
  16.2 4.5 %fusion.97 = (f32[4,64,3,1279]{3,1,2,0:T(8,128)}, f32[4,64,3,1279]{3,1,2,0:T(8,128)}) fusion(f32[4,64,3,1280]{3,1,2,0:T(8,128)S(1)} %bitcast.99), kind=kLoop, calls=%fused_computation.174 | loop fusion | bytes 15716352 | tf_op jit(solution)/shard_map/slice | solution.py:33
  20.8 4.5 %fusion.98 = (f32[4,64,3,1216]{3,1,2,0:T(8,128)}, f32[4,64,3,1216]{3,1,2,0:T(8,128)}) fusion(f32[4,64,3,1280]{3,1,2,0:T(8,128)S(1)} %bitcast.100), kind=kLoop, calls=%fused_computation.175 | loop fusion | bytes 14942208 | tf_op jit(solution)/shard_map/slice | solution.py:33
  25.3 0.0 copy-done.18
  25.3 0.1 reshape.242
  25.4 0.0 copy-done
  25.4 0.8 gather_fusion
  26.1 0.1 reshape.241
  26.2 0.0 copy-done.19
  26.3 0.6 dynamic_slice.10
  27.4 0.1 broadcast_in_dim.25
  27.5 0.1 dynamic-slice
  27.6 0.0 all-to-all-done
  27.7 0.6 gather_fusion.1
  28.3 0.1 dynamic-slice_select_fusion
  28.5 0.3 collective-permute-done.1
  28.8 6.6 %collective-permute-done = f32[4,64,1,1280]{3,1,2,0:T(8,128)} collective-permute-done((f32[4,64,1,1280]{3,1,2,0:T(8,128)S(1)}, f32[4,64,1,1280]{3,1,2,0:T(8,128)}, u32[]{:S(2)}, u32[]{:S(2)}) %collective-permute-start) | collective-permute-done | bytes 1310752 | tf_op jit(solution)/shard_map/ppermute | solution.py:25
  35.4 13.5 %multiply_subtract_fusion.2 = (f32[4,64,3,1280]{3,1,2,0:T(8,128)S(1)}, f32[4,64,3,1280]{3,1,2,0:T(8,128)}, f32[4,64,3,1280]{3,1,2,0:T(8,128)}) fusion(f32[4,64,3,1280]{3,1,2,0:T(8,128)} %bitcast.98, f32[4,64,3,1279]{3,1,2,0:T(8,128)} %get-tuple-element.38, f32[4,64,3,1279]{3,1,2,0:T(8,128)} %get-tuple-element.37, f32[4,64,3,1216]{3,1,2,0:T(8,128)} %get-tuple-element.40, ...), kind=kLoop, calls=%fused_computation.28 | loop fusion | flops 14745600 | bytes 33689600 | tf_op jit(solution)/shard_map/sub | solution.py:48
  48.9 0.0 copy-done.3
  48.9 0.0 copy-start.10
  48.9 0.0 copy-start.11
  48.9 3.5 %fusion.72 = (f32[1,64,3,1280]{3,1,2,0:T(8,128)S(1)}, f32[1,64,3,1280]{3,1,2,0:T(8,128)S(1)}) fusion(f32[4,64,3,1280]{3,1,2,0:T(8,128)} %get-tuple-element.22, f32[4,64,3,1280]{3,1,2,0:T(8,128)} %get-tuple-element.24, f32[4,64,3,1280]{3,1,2,0:T(8,128)S(1)} %get-tuple-element.21, f32[1,4,64,3,1280]{4,2,3,1,0:T(8,128)S(1)} %copy-done.3, ...), kind=kLoop, calls=%fused_computation.116 | loop fusion | flops 5898240 | bytes 11857920 | tf_op jit(solution)/shard_map/add | solution.py:67
  52.4 0.0 copy-done.10
  52.4 1.0 copy-done.11
  53.4 1.1 fusion.78
  54.5 0.6 broadcast_multiply_fusion
  55.1 0.2 fusion.96
  55.3 1.9 %collective-permute-start.3 = (f32[4,64,1,1280]{3,1,2,0:T(8,128)S(1)}, f32[4,64,1,1280]{3,1,2,0:T(8,128)S(1)}, u32[]{:S(2)}, u32[]{:S(2)}) collective-permute-start(f32[4,64,1,1280]{3,1,2,0:T(8,128)S(1)} %get-tuple-element.35), channel_id=1, source_target_pairs={{0,1},{1,2},{2,3},{3,4},{4,5},{5,6},{6,7},{7,8},{8,9},{9,10},{10,1... | collective-permute-start | bytes 3932168 | tf_op jit(solution)/shard_map/ppermute | solution.py:22
  57.2 2.6 %collective-permute-start.2 = (f32[4,64,1,1280]{3,1,2,0:T(8,128)S(1)}, f32[4,64,1,1280]{3,1,2,0:T(8,128)S(1)}, u32[]{:S(2)}, u32[]{:S(2)}) collective-permute-start(f32[4,64,1,1280]{3,1,2,0:T(8,128)S(1)} %get-tuple-element.36), channel_id=1, source_target_pairs={{1,0},{2,1},{3,2},{4,3},{5,4},{6,5},{7,6},{8,7},{9,8},{10,9},{11,1... | collective-permute-start | bytes 3932168 | tf_op jit(solution)/shard_map/ppermute | solution.py:25
  59.8 4.4 %fusion.94 = (f32[4,64,3,1279]{3,1,2,0:T(8,128)}, f32[4,64,3,1279]{3,1,2,0:T(8,128)}) fusion(f32[4,64,3,1280]{3,1,2,0:T(8,128)S(1)} %broadcast_multiply_fusion), kind=kLoop, calls=%fused_computation.171 | loop fusion | bytes 15716352 | tf_op jit(solution)/shard_map/slice | solution.py:33
  64.2 4.4 %fusion.95 = (f32[4,64,3,1216]{3,1,2,0:T(8,128)}, f32[4,64,3,1216]{3,1,2,0:T(8,128)}) fusion(f32[4,64,3,1280]{3,1,2,0:T(8,128)S(1)} %broadcast_multiply_fusion), kind=kLoop, calls=%fused_computation.172 | loop fusion | bytes 14942208 | tf_op jit(solution)/shard_map/slice | solution.py:33
  68.6 3.1 %collective-permute-done.3 = f32[4,64,1,1280]{3,1,2,0:T(8,128)S(1)} collective-permute-done((f32[4,64,1,1280]{3,1,2,0:T(8,128)S(1)}, f32[4,64,1,1280]{3,1,2,0:T(8,128)S(1)}, u32[]{:S(2)}, u32[]{:S(2)}) %collective-permute-start.3) | collective-permute-done | bytes 1310752 | tf_op jit(solution)/shard_map/ppermute | solution.py:22
  71.7 6.5 %collective-permute-done.2 = f32[4,64,1,1280]{3,1,2,0:T(8,128)S(1)} collective-permute-done((f32[4,64,1,1280]{3,1,2,0:T(8,128)S(1)}, f32[4,64,1,1280]{3,1,2,0:T(8,128)S(1)}, u32[]{:S(2)}, u32[]{:S(2)}) %collective-permute-start.2) | collective-permute-done | bytes 1310752 | tf_op jit(solution)/shard_map/ppermute | solution.py:25
  78.2 2.5 %subtract_multiply_fusion.2 = f32[4,64,3,1280]{3,1,2,0:T(8,128)} fusion(f32[4,64,1,1280]{3,1,2,0:T(8,128)S(1)} %collective-permute-done.2, f32[4,64,3,1280]{3,1,2,0:T(8,128)S(1)} %broadcast_multiply_fusion, f32[4,64,1,1280]{3,1,2,0:T(8,128)S(1)} %collective-permute-done.3), kind=kLoop, calls=%fused_computation.23 | loop fusion | flops 3932160 | bytes 10485760 | tf_op jit(solution)/shard_map/mul | solution.py:49
  80.7 9.3 %multiply_subtract_fusion.1 = (f32[4,64,3,1280]{3,1,2,0:T(8,128)}, f32[4,64,3,1280]{3,1,2,0:T(8,128)}) fusion(f32[4,64,3,1279]{3,1,2,0:T(8,128)} %get-tuple-element.32, f32[4,64,3,1279]{3,1,2,0:T(8,128)} %get-tuple-element.31, f32[4,64,3,1216]{3,1,2,0:T(8,128)} %get-tuple-element.34, f32[4,64,3,1216]{3,1,2,0:T(8,128)} %get-tuple-element.33, ...), kind=kLoop, calls=%fused_computation.25 | loop fusion | flops 17694720 | bytes 37621760 | tf_op jit(solution)/shard_map/sub | solution.py:48
  90.0 0.0 copy-start.6
  90.0 4.1 %fusion.48 = (f32[1,64,3,1280]{3,1,2,0:T(8,128)S(1)}, f32[1,64,3,1280]{3,1,2,0:T(8,128)S(1)}) fusion(f32[4,64,3,1280]{3,1,2,0:T(8,128)} %get-tuple-element.20, f32[4,64,3,1280]{3,1,2,0:T(8,128)} %subtract_multiply_fusion.2, f32[4,64,3,1280]{3,1,2,0:T(8,128)} %get-tuple-element.19, f32[4,64,3,1280]{3,1,2,0:T(8,128)S(1)} %broadcast_multiply_fusion, ...), kind=kLoop, calls=%fused_computation.84 | loop fusion | flops 5898240 | bytes 11857920 | tf_op jit(solution)/shard_map/add | solution.py:67
  94.1 1.0 copy-done.5
  95.1 1.1 copy-done.6
  96.2 1.0 fusion.54
  97.2 1.1 fusion.1
  98.3 0.1 copy-done.14
  98.4 0.2 fusion.93
  98.7 1.9 %collective-permute-start.5 = (f32[4,64,1,1280]{3,1,2,0:T(8,128)S(1)}, f32[4,64,1,1280]{3,1,2,0:T(8,128)S(1)}, u32[]{:S(2)}, u32[]{:S(2)}) collective-permute-start(f32[4,64,1,1280]{3,1,2,0:T(8,128)S(1)} %get-tuple-element.29), channel_id=1, source_target_pairs={{0,1},{1,2},{2,3},{3,4},{4,5},{5,6},{6,7},{7,8},{8,9},{9,10},{10,1... | collective-permute-start | bytes 3932168 | tf_op jit(solution)/shard_map/ppermute | solution.py:22
  100.6 2.6 %collective-permute-start.4 = (f32[4,64,1,1280]{3,1,2,0:T(8,128)S(1)}, f32[4,64,1,1280]{3,1,2,0:T(8,128)S(1)}, u32[]{:S(2)}, u32[]{:S(2)}) collective-permute-start(f32[4,64,1,1280]{3,1,2,0:T(8,128)S(1)} %get-tuple-element.30), channel_id=1, source_target_pairs={{1,0},{2,1},{3,2},{4,3},{5,4},{6,5},{7,6},{8,7},{9,8},{10,9},{11,1... | collective-permute-start | bytes 3932168 | tf_op jit(solution)/shard_map/ppermute | solution.py:25
  103.2 4.5 %fusion.92 = (f32[4,64,3,1216]{3,1,2,0:T(8,128)}, f32[4,64,3,1216]{3,1,2,0:T(8,128)}) fusion(f32[4,64,3,1280]{3,1,2,0:T(8,128)S(1)} %fusion.1), kind=kLoop, calls=%fused_computation.169 | loop fusion | bytes 14942208 | tf_op jit(solution)/shard_map/slice | solution.py:33
  107.7 4.5 %fusion.91 = (f32[4,64,3,1279]{3,1,2,0:T(8,128)}, f32[4,64,3,1279]{3,1,2,0:T(8,128)}) fusion(f32[4,64,3,1280]{3,1,2,0:T(8,128)S(1)} %fusion.1), kind=kLoop, calls=%fused_computation.168 | loop fusion | bytes 15716352 | tf_op jit(solution)/shard_map/slice | solution.py:33
  112.2 2.9 %collective-permute-done.5 = f32[4,64,1,1280]{3,1,2,0:T(8,128)S(1)} collective-permute-done((f32[4,64,1,1280]{3,1,2,0:T(8,128)S(1)}, f32[4,64,1,1280]{3,1,2,0:T(8,128)S(1)}, u32[]{:S(2)}, u32[]{:S(2)}) %collective-permute-start.5) | collective-permute-done | bytes 1310752 | tf_op jit(solution)/shard_map/ppermute | solution.py:22
  115.1 6.5 %collective-permute-done.4 = f32[4,64,1,1280]{3,1,2,0:T(8,128)S(1)} collective-permute-done((f32[4,64,1,1280]{3,1,2,0:T(8,128)S(1)}, f32[4,64,1,1280]{3,1,2,0:T(8,128)S(1)}, u32[]{:S(2)}, u32[]{:S(2)}) %collective-permute-start.4) | collective-permute-done | bytes 1310752 | tf_op jit(solution)/shard_map/ppermute | solution.py:25
  121.6 1.2 copy-done.17
  122.8 10.8 %multiply_subtract_fusion = (f32[4,64,3,1280]{3,1,2,0:T(8,128)}, f32[4,64,3,1280]{3,1,2,0:T(8,128)}, f32[4,64,3,1280]{3,1,2,0:T(8,128)}) fusion(f32[4,64,3,1280]{3,1,2,0:T(8,128)S(1)} %fusion.1, f32[4,64,3,1279]{3,1,2,0:T(8,128)} %get-tuple-element.26, f32[4,64,3,1279]{3,1,2,0:T(8,128)} %get-tuple-element.25, f32[4,64,3,1216]{3,1,2,0:T(8,128)} %get-tuple-element.28, ...), kind=kLoop, calls=%fused_computation.22 | loop fusion | flops 14745600 | bytes 33689600 | tf_op jit(solution)/shard_map/sub | solution.py:48
  133.6 4.1 %fusion.23 = (f32[1,1,64,3,1280]{4,2,3,1,0:T(8,128)S(1)}, f32[1,1,64,3,1280]{4,2,3,1,0:T(8,128)S(1)}) fusion(f32[4,64,3,1280]{3,1,2,0:T(8,128)} %get-tuple-element.18, f32[4,64,3,1280]{3,1,2,0:T(8,128)} %get-tuple-element.23, f32[4,64,3,1280]{3,1,2,0:T(8,128)} %get-tuple-element.17, f32[4,64,3,1280]{3,1,2,0:T(8,128)S(1)} %fusion.1, ...), kind=kLoop, calls=%fused_computation.51 | loop fusion | flops 5898240 | bytes 11857920 | tf_op jit(solution)/shard_map/stack | solution.py:90
  137.7 1.0 copy-done.8
  138.7 1.1 copy-done.9
  139.8 2.0 %fusion.30 = (f32[1,1,64,3,1280]{4,2,3,1,0:T(8,128)S(1)}, f32[1,1,64,3,1280]{4,2,3,1,0:T(8,128)}) fusion(f32[4,64,3,1280]{3,1,2,0:T(8,128)S(1)} %copy-done.9, f32[4,64,3,1280]{3,1,2,0:T(8,128)S(1)} %copy-done.8, f32[4,64,3,1280]{3,1,2,0:T(8,128)S(1)} %copy-done.7, f32[4,64,3,1280]{3,1,2,0:T(8,128)S(1)} %fusion.1, f32[3,1280]{1,0:T(4,128)S(1)} %get-tuple-element.49, ...), kind=kLoop, calls=%fused_computation.60 | loop fusion | flops 5898240 | bytes 11857920 | tf_op jit(solution)/shard_map/stack | solution.py:90
  141.8 0.0 copy-done.15
  141.8 4.5 %fusion.3 = f32[1,4,64,3,1280]{4,2,3,1,0:T(8,128)} fusion(f32[1,1,64,3,1280]{4,2,3,1,0:T(8,128)} %get-tuple-element.6, f32[1,1,64,3,1280]{4,2,3,1,0:T(8,128)S(1)} %get-tuple-element.8, f32[1,1,64,3,1280]{4,2,3,1,0:T(8,128)S(1)} %get-tuple-element.7, f32[1,1,64,3,1280]{4,2,3,1,0:T(8,128)S(1)} %get-tuple-element.5, f32[1,1,64,3,1280]{4,2,3,1,0:T(8,128)S(1)} %bitcast.108, ...), kind=kLoop, calls=%fused_computation.14 | loop fusion | flops 20643840 | bytes 19660800 | tf_op jit(solution)/shard_map/sub | solution.py:116
  (34 shorter events, 0.2 us)
Async XLA Ops:
  0.0 25.4 %copy-start = (s32[32]{0:T(128)S(1)}, s32[32]{0:T(128)}, u32[]{:S(2)}) copy-start(s32[32]{0:T(128)} %param.8) | copy-start | bytes 388
  1.7 25.9 %all-to-all-start = ((f32[8,4,3,4,256]{4,1,3,2,0:T(4,128)}), f32[8,4,3,4,256]{4,1,3,2,0:T(4,128)S(1)}, u32[]{:S(2)}, u32[]{:S(2)}) async-start(f32[8,4,3,4,256]{4,1,3,2,0:T(4,128)} %stack.60), calls=%async_computation | async-start | bytes 786432 | tf_op jit(solution)/shard_map/all_to_all | solution.py:104
  9.0 7.2 %copy-start.2 = (f32[1,4,64,3,1280]{4,2,3,1,0:T(8,128)S(1)}, f32[1,4,64,3,1280]{4,2,3,1,0:T(8,128)}, u32[]{:S(2)}) copy-start(f32[1,4,64,3,1280]{4,2,3,1,0:T(8,128)} %param.5) | copy-start | bytes 11796484
  11.1 17.7 %collective-permute-start.1 = (f32[4,64,1,1280]{3,1,2,0:T(8,128)S(1)}, f32[4,64,1,1280]{3,1,2,0:T(8,128)}, u32[]{:S(2)}, u32[]{:S(2)}) collective-permute-start(f32[4,64,1,1280]{3,1,2,0:T(8,128)S(1)} %get-tuple-element.41), channel_id=1, source_target_pairs={{0,1},{1,2},{2,3},{3,4},{4,5},{5,6},{6,7},{7,8},{8,9},{9,10},{10,1... | collective-permute-start | bytes 3932168 | tf_op jit(solution)/shard_map/ppermute | solution.py:22
  14.3 21.1 %collective-permute-start = (f32[4,64,1,1280]{3,1,2,0:T(8,128)S(1)}, f32[4,64,1,1280]{3,1,2,0:T(8,128)}, u32[]{:S(2)}, u32[]{:S(2)}) collective-permute-start(f32[4,64,1,1280]{3,1,2,0:T(8,128)S(1)} %get-tuple-element.42), channel_id=1, source_target_pairs={{1,0},{2,1},{3,2},{4,3},{5,4},{6,5},{7,6},{8,7},{9,8},{10,9},{11,1... | collective-permute-start | bytes 3932168 | tf_op jit(solution)/shard_map/ppermute | solution.py:25
  20.8 4.5 %copy-start.18 = (s32[8,6]{1,0:T(8,128)S(1)}, s32[8,6]{1,0:T(8,128)}, u32[]{:S(2)}) copy-start(s32[8,6]{1,0:T(8,128)} %param.7) | copy-start | bytes 580
  25.3 1.0 copy-start.19
  35.4 13.5 %copy-start.3 = (f32[1,4,64,3,1280]{4,2,3,1,0:T(8,128)S(1)}, f32[1,4,64,3,1280]{4,2,3,1,0:T(8,128)}, u32[]{:S(2)}) copy-start(f32[1,4,64,3,1280]{4,2,3,1,0:T(8,128)} %param.5) | copy-start | bytes 11796484
  48.9 3.5 %copy-start.10 = (f32[4,64,3,1280]{3,1,2,0:T(8,128)S(1)}, f32[4,64,3,1280]{3,1,2,0:T(8,128)}, u32[]{:S(2)}) copy-start(f32[4,64,3,1280]{3,1,2,0:T(8,128)} %get-tuple-element.22) | copy-start | bytes 11796484
  48.9 4.5 %copy-start.11 = (f32[4,64,3,1280]{3,1,2,0:T(8,128)S(1)}, f32[4,64,3,1280]{3,1,2,0:T(8,128)}, u32[]{:S(2)}) copy-start(f32[4,64,3,1280]{3,1,2,0:T(8,128)} %get-tuple-element.24) | copy-start | bytes 11796484
  55.3 16.5 %collective-permute-start.3 = (f32[4,64,1,1280]{3,1,2,0:T(8,128)S(1)}, f32[4,64,1,1280]{3,1,2,0:T(8,128)S(1)}, u32[]{:S(2)}, u32[]{:S(2)}) collective-permute-start(f32[4,64,1,1280]{3,1,2,0:T(8,128)S(1)} %get-tuple-element.35), channel_id=1, source_target_pairs={{0,1},{1,2},{2,3},{3,4},{4,5},{5,6},{6,7},{7,8},{8,9},{9,10},{10,1... | collective-permute-start | bytes 3932168 | tf_op jit(solution)/shard_map/ppermute | solution.py:22
  57.2 21.0 %collective-permute-start.2 = (f32[4,64,1,1280]{3,1,2,0:T(8,128)S(1)}, f32[4,64,1,1280]{3,1,2,0:T(8,128)S(1)}, u32[]{:S(2)}, u32[]{:S(2)}) collective-permute-start(f32[4,64,1,1280]{3,1,2,0:T(8,128)S(1)} %get-tuple-element.36), channel_id=1, source_target_pairs={{1,0},{2,1},{3,2},{4,3},{5,4},{6,5},{7,6},{8,7},{9,8},{10,9},{11,1... | collective-permute-start | bytes 3932168 | tf_op jit(solution)/shard_map/ppermute | solution.py:25
  90.0 4.1 %copy-start.4 = (f32[4,64,3,1280]{3,1,2,0:T(8,128)S(1)}, f32[4,64,3,1280]{3,1,2,0:T(8,128)}, u32[]{:S(2)}) copy-start(f32[4,64,3,1280]{3,1,2,0:T(8,128)} %subtract_multiply_fusion.2) | copy-start | bytes 11796484
  90.0 5.1 %copy-start.5 = (f32[4,64,3,1280]{3,1,2,0:T(8,128)S(1)}, f32[4,64,3,1280]{3,1,2,0:T(8,128)}, u32[]{:S(2)}) copy-start(f32[4,64,3,1280]{3,1,2,0:T(8,128)} %get-tuple-element.19) | copy-start | bytes 11796484
  90.0 6.2 %copy-start.6 = (f32[4,64,3,1280]{3,1,2,0:T(8,128)S(1)}, f32[4,64,3,1280]{3,1,2,0:T(8,128)}, u32[]{:S(2)}) copy-start(f32[4,64,3,1280]{3,1,2,0:T(8,128)} %get-tuple-element.20) | copy-start | bytes 11796484
  97.2 1.2 copy-start.12
  97.2 1.2 copy-start.14
  98.7 16.5 %collective-permute-start.5 = (f32[4,64,1,1280]{3,1,2,0:T(8,128)S(1)}, f32[4,64,1,1280]{3,1,2,0:T(8,128)S(1)}, u32[]{:S(2)}, u32[]{:S(2)}) collective-permute-start(f32[4,64,1,1280]{3,1,2,0:T(8,128)S(1)} %get-tuple-element.29), channel_id=1, source_target_pairs={{0,1},{1,2},{2,3},{3,4},{4,5},{5,6},{6,7},{7,8},{8,9},{9,10},{10,1... | collective-permute-start | bytes 3932168 | tf_op jit(solution)/shard_map/ppermute | solution.py:22
  100.6 21.0 %collective-permute-start.4 = (f32[4,64,1,1280]{3,1,2,0:T(8,128)S(1)}, f32[4,64,1,1280]{3,1,2,0:T(8,128)S(1)}, u32[]{:S(2)}, u32[]{:S(2)}) collective-permute-start(f32[4,64,1,1280]{3,1,2,0:T(8,128)S(1)} %get-tuple-element.30), channel_id=1, source_target_pairs={{1,0},{2,1},{3,2},{4,3},{5,4},{6,5},{7,6},{8,7},{9,8},{10,9},{11,1... | collective-permute-start | bytes 3932168 | tf_op jit(solution)/shard_map/ppermute | solution.py:25
  115.1 6.5 %copy-start.16 = (f32[4,64,1,1280]{3,1,2,0:T(8,128)}, f32[4,64,1,1280]{3,1,2,0:T(8,128)S(1)}, u32[]{:S(2)}) copy-start(f32[4,64,1,1280]{3,1,2,0:T(8,128)S(1)} %collective-permute-done.5) | copy-start | bytes 3932164
  121.6 1.2 copy-start.17
  133.6 4.1 %copy-start.7 = (f32[4,64,3,1280]{3,1,2,0:T(8,128)S(1)}, f32[4,64,3,1280]{3,1,2,0:T(8,128)}, u32[]{:S(2)}) copy-start(f32[4,64,3,1280]{3,1,2,0:T(8,128)} %get-tuple-element.17) | copy-start | bytes 11796484
  133.6 5.1 %copy-start.8 = (f32[4,64,3,1280]{3,1,2,0:T(8,128)S(1)}, f32[4,64,3,1280]{3,1,2,0:T(8,128)}, u32[]{:S(2)}) copy-start(f32[4,64,3,1280]{3,1,2,0:T(8,128)} %get-tuple-element.18) | copy-start | bytes 11796484
  133.6 6.2 %copy-start.9 = (f32[4,64,3,1280]{3,1,2,0:T(8,128)S(1)}, f32[4,64,3,1280]{3,1,2,0:T(8,128)}, u32[]{:S(2)}) copy-start(f32[4,64,3,1280]{3,1,2,0:T(8,128)} %get-tuple-element.23) | copy-start | bytes 11796484
  139.8 2.0 %copy-start.13 = (f32[1,64,3,1280]{3,1,2,0:T(8,128)S(1)}, f32[1,64,3,1280]{3,1,2,0:T(8,128)}, u32[]{:S(2)}) copy-start(f32[1,64,3,1280]{3,1,2,0:T(8,128)} %copy-done.12) | copy-start | bytes 2949124
  139.8 2.0 %copy-start.15 = (f32[1,64,3,1280]{3,1,2,0:T(8,128)S(1)}, f32[1,64,3,1280]{3,1,2,0:T(8,128)}, u32[]{:S(2)}) copy-start(f32[1,64,3,1280]{3,1,2,0:T(8,128)} %copy-done.14) | copy-start | bytes 2949124
  141.8 4.5 %copy-start.1 = (s32[32]{0:T(128)S(1)}, s32[32]{0:T(128)}, u32[]{:S(2)}) copy-start(s32[32]{0:T(128)} %param.8) | copy-start | bytes 388
